TPU v7x, 128 devices: a whole 4x4x4 slice. The times are simulated.
128 devices in a mesh: dof: 32 (over x, z, core), snap: 4 (over y).
Axes of the slice: x: 4, y: 4, z: 4, core: 2. Of those that a mesh axis runs over, the one named last changes fastest.
Arguments:
- snapshots: bfloat16 [131072, 1024], P('dof', 'snap')
- lengths: int32 [16], replicated, may hold values from 16 to 64, as said below
- start_block: float32 [1024, 128], replicated, may hold values from -6 to 6
Outputs:
- pod_modes: float32 [131072, 128], P(('dof', 'snap'))
- r_factor: float32 [1024, 1024], replicated
Inputs may be any that keep to these rules, and one draw needn't show every extreme that they name: `lengths`: some passage has all 64 steps active and some passage only a quarter of them.
All inputs are finite; a program needn't handle non-finite values.
Results may differ from a plain program's by a relative error of at most 0.0003.
Values may be sent and summed in bfloat16 or wider, within the bound.
No kernel may reach another device: no remote copies, remote signals or barrier semaphores. Data moves between devices by JAX's collectives and lax.ppermute only.
A program may use at most 128 MiB of HBM per device.

v0:
```python
import jax
import jax.numpy as jnp
from jax import lax
from jax.sharding import PartitionSpec as P

STEPS = 64
ITERS = 3
PASSES = 16
TILE = 128


def pack_upper(rows):
    width = rows.shape[1]
    pieces = []
    for i in range(width // TILE):
        lhs = rows[:, i * TILE : (i + 1) * TILE]
        rhs = rows[:, i * TILE :]
        pieces.append(
            lax.dot_general(lhs, rhs, (((0,), (0,)), ((), ())), preferred_element_type=jnp.float32)
        )
    return jnp.concatenate(pieces, axis=1)


def unpack_upper(packed, width):
    blocks = width // TILE
    upper_rows = []
    offset = 0
    for i in range(blocks):
        w = width - i * TILE
        piece = packed[:, offset : offset + w]
        offset += w
        upper_rows.append(jnp.pad(piece, ((0, 0), (i * TILE, 0))))
    upper = jnp.concatenate(upper_rows, axis=0)
    r = lax.broadcasted_iota(jnp.int32, (width, width), 0) // TILE
    c = lax.broadcasted_iota(jnp.int32, (width, width), 1) // TILE
    return jnp.where(r <= c, upper, upper.T)


def body(snapshots, lengths, start_block):
    rows = lax.all_to_all(snapshots, "snap", 0, 1, tiled=True)
    width = rows.shape[1]
    col_length = jnp.repeat(lengths, STEPS, total_repeat_length=width)
    columns = jnp.arange(width, dtype=jnp.int32)
    active = columns % STEPS < col_length
    masked = jnp.where(active[None, :], rows, jnp.zeros_like(rows))
    row_count = snapshots.shape[0] * lax.axis_size("dof")
    packed = lax.psum(pack_upper(masked), ("dof", "snap"))
    gram_sum = unpack_upper(packed, width)
    shifted = gram_sum / jnp.float32(row_count) + 0.05 * jnp.eye(width, dtype=jnp.float32)
    upper_factor = lax.linalg.cholesky(shifted, symmetrize_input=False).T
    contract = (((0,), (0,)), ((), ()))
    subspace = start_block
    for sweep in range(ITERS):
        image = jnp.dot(
            shifted, subspace, precision=lax.Precision.HIGHEST, preferred_element_type=jnp.float32
        )
        correlation = lax.dot_general(
            image,
            image,
            contract,
            precision=lax.Precision.HIGHEST,
            preferred_element_type=jnp.float32,
        )
        lower_factor = jnp.linalg.cholesky(correlation)
        subspace = lax.linalg.triangular_solve(
            lower_factor, image, left_side=False, lower=True, transpose_a=True
        )
    pod_modes = jnp.dot(
        masked.astype(jnp.float32),
        subspace,
        precision=lax.Precision.HIGHEST,
        preferred_element_type=jnp.float32,
    )
    return (pod_modes, upper_factor)


def solution(mesh):
    placed = (P("dof", "snap"), P(), P())
    return jax.shard_map(
        body, mesh=mesh, in_specs=placed, out_specs=(P(("dof", "snap"), None), P()), check_vma=False
    )
```

profile of v0, /device:TPU:1, one launch (start us, length us, event | category | flops | bytes accessed | tf_op | source)
XLA Modules:
  0.0 540.3 jit_solution(2373709611297239090)
XLA Ops:
  7.2 5.2 all-to-all-start
  13.2 4.4 compare_select_fusion.1
  17.7 5.7 %fusion.98 = pred[1024]{0:T(1024)(128)(4,1)S(1)} fusion(pred[1024]{0:T(1024)(128)(4,1)S(1)} %get-tuple-element.30, pred[1024]{0:T(1024)(128)(4,1)S(1)} %get-tuple-element.29, pred[1024]{0:T(1024)(128)(4,1)S(1)} %get-tuple-element.28, pred[1024]{0:T(1024)(128)(4,1)S(1)} %get-tuple-element.27, pred[1024]{0:T(1024)(128)(4,1)S(1)} %get-tuple-element.26, ...), kind=kLoop, calls=%fused_computation.159 | loop fusion | flops 25600 | bytes 18500 | tf_op jit(solution)/shard_map/lt | solution.py:44
  23.4 14.4 %all-to-all-done = bf16[4,1024,256]{2,1,0:T(8,128)(2,1)S(1)} async-done(((bf16[4,1024,256]{2,1,0:T(8,128)(2,1)}), bf16[4,1024,256]{2,1,0:T(8,128)(2,1)S(1)}, u32[]{:S(2)}, u32[]{:S(2)}) %all-to-all-start) | async-done | bytes 2097184 | tf_op jit(solution)/shard_map/all_to_all | solution.py:40
  37.8 2.4 copy.29
  40.1 1.8 bitcast_select_fusion.1
  42.0 1.5 convolution_dynamic-update-slice_fusion
  51.5 152.8 %all-reduce.10.cloned.1.call-done = f32[128,4608]{0,1:T(8,128)} async-done(((f32[128,4608]{0,1:T(8,128)}), f32[128,4608]{0,1:T(8,128)}) %all-reduce.10.cloned.1.call-update) | async-done | bytes 2359312 | tf_op jit(solution)/shard_map/psum | solution.py:47
  205.4 1.9 slice_dynamic-update-slice_fusion
  214.1 5.3 copy.37
  219.5 4.2 fusion.1
  223.7 2.0 copy-done.1
  225.7 11.7 %cholesky.247 = f32[128,128]{1,0:T(8,128)S(1)} custom-call(f32[128,128]{1,0:T(8,128)S(1)} %cholesky.667), custom_call_target="Cholesky" | custom-call | tf_op jit(solution)/shard_map/cholesky | solution.py:50
  238.1 9.8 %custom-call.49 = f32[1,128,128]{1,2,0:T(8,128)S(1)} custom-call(f32[1,128,128]{2,1,0:T(8,128)S(1)} %get-tuple-element.54), custom_call_target="InvertDiagBlocksLowerTriangular" | custom-call | tf_op jit(solution)/shard_map/cholesky | solution.py:50
  247.9 5.4 fusion.106
  254.5 11.7 %cholesky.636 = f32[128,128]{1,0:T(8,128)S(1)} custom-call(f32[128,128]{1,0:T(8,128)S(1)} %fusion.63), custom_call_target="Cholesky" | custom-call | tf_op jit(solution)/shard_map/jit(cholesky)/cholesky | solution.py:64
  267.5 9.8 %custom-call.58 = f32[1,128,128]{1,2,0:T(8,128)S(1)} custom-call(f32[1,128,128]{2,1,0:T(8,128)S(1)} %fusion.46), custom_call_target="InvertDiagBlocksLowerTriangular" | custom-call | tf_op jit(solution)/shard_map/triangular_solve/custom-call.16 | solution.py:65
  278.0 5.4 %fusion.108 = f32[1024,128]{1,0:T(8,128)S(1)} fusion(f32[1024,1024]{1,0:T(8,128)} %copy-done.1, f32[1024,128]{0,1:T(8,128)S(1)} %convolution_bitcast_fusion.2), kind=kOutput, calls=%fused_computation.192 | convolution fusion | flops 1610612736 | bytes 5242880 | tf_op jit(solution)/shard_map/dot_general | solution.py:54
  284.6 11.7 %cholesky.647 = f32[128,128]{1,0:T(8,128)S(1)} custom-call(f32[128,128]{1,0:T(8,128)S(1)} %fusion.61), custom_call_target="Cholesky" | custom-call | tf_op jit(solution)/shard_map/jit(cholesky)/cholesky | solution.py:64
  297.6 9.8 %custom-call.59 = f32[1,128,128]{1,2,0:T(8,128)S(1)} custom-call(f32[1,128,128]{2,1,0:T(8,128)S(1)} %fusion.47), custom_call_target="InvertDiagBlocksLowerTriangular" | custom-call | tf_op jit(solution)/shard_map/triangular_solve/custom-call.16 | solution.py:65
  308.1 5.6 %fusion.110 = f32[1024,128]{1,0:T(8,128)S(1)} fusion(f32[1024,1024]{1,0:T(8,128)} %copy-done.1, f32[1024,128]{0,1:T(8,128)S(1)} %convolution_bitcast_fusion.1), kind=kOutput, calls=%fused_computation.194 | convolution fusion | flops 1610612736 | bytes 5242880 | tf_op jit(solution)/shard_map/dot_general | solution.py:54
  314.8 11.7 %cholesky.658 = f32[128,128]{1,0:T(8,128)S(1)} custom-call(f32[128,128]{1,0:T(8,128)S(1)} %fusion.59), custom_call_target="Cholesky" | custom-call | tf_op jit(solution)/shard_map/jit(cholesky)/cholesky | solution.py:64
  327.9 9.8 %custom-call.60 = f32[1,128,128]{1,2,0:T(8,128)S(1)} custom-call(f32[1,128,128]{2,1,0:T(8,128)S(1)} %fusion.48), custom_call_target="InvertDiagBlocksLowerTriangular" | custom-call | tf_op jit(solution)/shard_map/triangular_solve/custom-call.16 | solution.py:65
  338.4 3.1 fusion.112
  341.5 2.5 cholesky.279
  343.9 2.4 constant_dynamic-update-slice_fusion.6
  346.3 1.5 convolution_subtract_fusion
  347.9 11.9 %cholesky.270 = f32[128,128]{1,0:T(8,128)S(1)} custom-call(f32[128,128]{1,0:T(8,128)S(1)} %cholesky.671), custom_call_target="Cholesky" | custom-call | tf_op jit(solution)/shard_map/cholesky | solution.py:50
  361.1 9.8 %custom-call.50 = f32[1,128,128]{1,2,0:T(8,128)S(1)} custom-call(f32[1,128,128]{2,1,0:T(8,128)S(1)} %get-tuple-element.51), custom_call_target="InvertDiagBlocksLowerTriangular" | custom-call | tf_op jit(solution)/shard_map/cholesky | solution.py:50
  372.2 2.1 convolution_subtract_fusion.1
  374.3 11.7 %cholesky.493 = f32[128,128]{1,0:T(8,128)S(1)} custom-call(f32[128,128]{1,0:T(8,128)S(1)} %cholesky.676), custom_call_target="Cholesky" | custom-call | tf_op jit(solution)/shard_map/cholesky | solution.py:50
  387.3 10.0 %custom-call.51 = f32[1,128,128]{1,2,0:T(8,128)S(1)} custom-call(f32[1,128,128]{2,1,0:T(8,128)S(1)} %get-tuple-element.48), custom_call_target="InvertDiagBlocksLowerTriangular" | custom-call | tf_op jit(solution)/shard_map/cholesky | solution.py:50
  398.5 2.3 convolution_subtract_fusion.2
  400.9 11.7 %cholesky.512 = f32[128,128]{1,0:T(8,128)S(1)} custom-call(f32[128,128]{1,0:T(8,128)S(1)} %cholesky.681), custom_call_target="Cholesky" | custom-call | tf_op jit(solution)/shard_map/cholesky | solution.py:50
  413.9 9.8 %custom-call.52 = f32[1,128,128]{1,2,0:T(8,128)S(1)} custom-call(f32[1,128,128]{2,1,0:T(8,128)S(1)} %get-tuple-element.45), custom_call_target="InvertDiagBlocksLowerTriangular" | custom-call | tf_op jit(solution)/shard_map/cholesky | solution.py:50
  424.8 2.3 convolution_subtract_fusion.3
  427.1 12.1 %cholesky.531 = f32[128,128]{1,0:T(8,128)S(1)} custom-call(f32[128,128]{1,0:T(8,128)S(1)} %cholesky.686), custom_call_target="Cholesky" | custom-call | tf_op jit(solution)/shard_map/cholesky | solution.py:50
  440.5 9.8 %custom-call.53 = f32[1,128,128]{1,2,0:T(8,128)S(1)} custom-call(f32[1,128,128]{2,1,0:T(8,128)S(1)} %get-tuple-element.42), custom_call_target="InvertDiagBlocksLowerTriangular" | custom-call | tf_op jit(solution)/shard_map/cholesky | solution.py:50
  451.3 2.3 convolution_subtract_fusion.4
  453.6 11.7 %cholesky.551 = f32[128,128]{1,0:T(8,128)S(1)} custom-call(f32[128,128]{1,0:T(8,128)S(1)} %cholesky.691), custom_call_target="Cholesky" | custom-call | tf_op jit(solution)/shard_map/cholesky | solution.py:50
  466.7 9.8 %custom-call.54 = f32[1,128,128]{1,2,0:T(8,128)S(1)} custom-call(f32[1,128,128]{2,1,0:T(8,128)S(1)} %get-tuple-element.39), custom_call_target="InvertDiagBlocksLowerTriangular" | custom-call | tf_op jit(solution)/shard_map/cholesky | solution.py:50
  477.4 2.0 convolution_subtract_fusion.5
  479.5 11.9 %cholesky.571 = f32[128,128]{1,0:T(8,128)S(1)} custom-call(f32[128,128]{1,0:T(8,128)S(1)} %cholesky.696), custom_call_target="Cholesky" | custom-call | tf_op jit(solution)/shard_map/cholesky | solution.py:50
  492.6 9.8 %custom-call.55 = f32[1,128,128]{1,2,0:T(8,128)S(1)} custom-call(f32[1,128,128]{2,1,0:T(8,128)S(1)} %get-tuple-element.36), custom_call_target="InvertDiagBlocksLowerTriangular" | custom-call | tf_op jit(solution)/shard_map/cholesky | solution.py:50
  503.3 1.8 convolution_subtract_fusion.6
  505.1 11.7 %cholesky.589 = f32[128,128]{1,0:T(8,128)S(1)} custom-call(f32[128,128]{1,0:T(8,128)S(1)} %convolution_subtract_fusion.6), custom_call_target="Cholesky" | custom-call | tf_op jit(solution)/shard_map/cholesky | solution.py:50
  523.1 4.8 select_bitcast_fusion
  527.9 5.3 copy.41
  (91 shorter events, 42.4 us)
Async XLA Ops:
  7.2 240.8 %copy-start = (f32[1024,128]{1,0:T(8,128)S(1)}, f32[1024,128]{1,0:T(8,128)}, u32[]{:S(2)}) copy-start(f32[1024,128]{1,0:T(8,128)} %param.10) | copy-start | bytes 1572868
  7.2 5.9 %copy-start.3 = (s32[8,128]{1,0:T(8,128)S(1)}, s32[8,128]{1,0:T(8,128)}, u32[]{:S(2)}) copy-start(s32[8,128]{1,0:T(8,128)} %constant.336.clone.1) | copy-start | bytes 12292
  7.2 5.2 copy-start.2
  7.2 30.6 %all-to-all-start = ((bf16[4,1024,256]{2,1,0:T(8,128)(2,1)}), bf16[4,1024,256]{2,1,0:T(8,128)(2,1)S(1)}, u32[]{:S(2)}, u32[]{:S(2)}) async-start(bf16[4,1024,256]{2,1,0:T(8,128)(2,1)} %bitcast.129), calls=%async_computation | async-start | bytes 4194304 | tf_op jit(solution)/shard_map/all_to_all | solution.py:40
  12.4 191.9 %all-reduce.10.cloned.1.call-start = ((), (), s32[]{:S(2)}) async-start(), calls=%async_computation.1 | async-start | bytes 4718592 | tf_op jit(solution)/shard_map/psum | solution.py:47
  204.3 5.7 %slice-start = ((f32[128,4608]{0,1:T(8,128)}), f32[128,640]{0,1:T(8,128)S(1)}, s32[]{:S(2)}) async-start(f32[128,4608]{0,1:T(8,128)} %all-reduce.10.cloned.1.call-done), calls=%async_computation.2 | async-start | bytes 655360 | tf_op jit(solution)/shard_map/slice | solution.py:30
  204.3 6.6 %slice-start.1 = ((f32[128,4608]{0,1:T(8,128)}), f32[128,512]{0,1:T(8,128)S(1)}, s32[]{:S(2)}) async-start(f32[128,4608]{0,1:T(8,128)} %all-reduce.10.cloned.1.call-done), calls=%async_computation.3 | async-start | bytes 524288 | tf_op jit(solution)/shard_map/slice | solution.py:30
  204.3 7.4 %slice-start.2 = ((f32[128,4608]{0,1:T(8,128)}), f32[128,384]{0,1:T(8,128)S(1)}, s32[]{:S(2)}) async-start(f32[128,4608]{0,1:T(8,128)} %all-reduce.10.cloned.1.call-done), calls=%async_computation.4 | async-start | bytes 393216 | tf_op jit(solution)/shard_map/slice | solution.py:30
  205.4 7.1 %slice-start.3 = ((f32[128,4608]{0,1:T(8,128)}), f32[128,256]{0,1:T(8,128)S(1)}, s32[]{:S(2)}) async-start(f32[128,4608]{0,1:T(8,128)} %all-reduce.10.cloned.1.call-done), calls=%async_computation.5 | async-start | bytes 262144 | tf_op jit(solution)/shard_map/slice | solution.py:30
  205.4 7.9 %slice-start.4 = ((f32[128,4608]{0,1:T(8,128)}), f32[128,128]{0,1:T(8,128)S(1)}, s32[]{:S(2)}) async-start(f32[128,4608]{0,1:T(8,128)} %all-reduce.10.cloned.1.call-done), calls=%async_computation.6 | async-start | bytes 131072 | tf_op jit(solution)/shard_map/slice | solution.py:30
  223.7 2.0 copy-start.1
Sparse Core Ops, SparseCore 0:
  51.6 152.6 all-reduce.9
where the time goes:
time: 549 us; the launch traced here: 540 us
  other arithmetic  263 us (48%)
  waiting for transfers between devices  167 us (30%)
  matrix products  57.1 us (10%)
  local copies, waits for them, and re-layouts  28.4 us (5%)
  between operations  19.6 us (4%)
    another operation x31, other arithmetic, body(): upper_factor = lax.linalg.cholesky(shifted, symmetrize_input=False).T  173 us
    psum x1, waiting for transfers between devices, body(): packed = lax.psum(pack_upper(masked), ('dof', 'snap'))  153 us
    another operation x9, other arithmetic, body(): lower_factor = jnp.linalg.cholesky(correlation)  37.2 us
    another operation x6, other arithmetic, body(): lax.linalg.triangular_solve(lower_factor, image, left_side=False, lower=T...  31.4 us
    another operation x14, matrix products, body(): upper_factor = lax.linalg.cholesky(shifted, symmetrize_input=False).T  23.1 us
    dot_general x3, matrix products, body(): jnp.dot(shifted, subspace, precision=lax.Precision.HIGHEST, preferred_ele...  16.4 us
    all_to_all x1, waiting for transfers between devices, body(): rows = lax.all_to_all(snapshots, 'snap', 0, 1, tiled=True)  14.4 us
    unnamed x16, local copies, waits for them, and re-layouts  14.2 us
  transfers between devices with their start and end apart: 2, of which 2 were waited for; matrix products, arithmetic and copies ran while one was open for 2% of the time, Pallas kernels for 0%

commit v1 on v0

--- a/solution.py
+++ b/solution.py
@@ -7,6 +7,18 @@
 ITERS = 3
 PASSES = 16
 TILE = 128
+
+
+def cut_along(x, dim, size):
+    dims = x.shape
+    pieces = x.reshape(*dims[:dim], size, dims[dim] // size, *dims[dim + 1 :])
+    return jnp.moveaxis(pieces, dim, 0)
+
+
+def joined_along(parts, dim):
+    parts = jnp.moveaxis(parts, 0, dim)
+    shape = parts.shape
+    return parts.reshape(*shape[:dim], shape[dim] * shape[dim + 1], *shape[dim + 2 :])
 
 
 def pack_upper(rows):
@@ -37,7 +49,14 @@
 
 
 def body(snapshots, lengths, start_block):
-    rows = lax.all_to_all(snapshots, "snap", 0, 1, tiled=True)
+    size, place = (lax.axis_size("snap"), lax.axis_index("snap"))
+    parts = cut_along(snapshots, 0, size)
+    outs = [parts[place]]
+    for step in range(1, size):
+        sent = parts[place ^ step]
+        outs.append(lax.ppermute(sent, "snap", [(i_2, i_2 ^ step) for i_2 in range(size)]))
+    parts = jnp.stack(outs)[place ^ jnp.arange(size)]
+    rows = joined_along(parts, 1)
     width = rows.shape[1]
     col_length = jnp.repeat(lengths, STEPS, total_repeat_length=width)
     columns = jnp.arange(width, dtype=jnp.int32)

time: 549 us -> 554 us (level)
    all_to_all x1 -> x0, waiting for transfers between devices: 14.4 us -> none  [body(): rows = lax.all_to_all(snapshots, 'snap', 0, 1, tiled=True)]
    ppermute x0 -> x3, waiting for transfers between devices: none -> 11.5 us  [body(): lax.ppermute(sent, 'snap', [(i_2, i_2 ^ step) for i_2 in range(size)])]
  transfers between devices with their start and end apart: 2 -> 4, of which waited for: 2 -> 3; matrix products, arithmetic and copies ran while one was open for 2% -> 2% of each run, Pallas kernels for 0% -> 0%
where the time goes in v1:
time: 554 us; the launch traced here: 544 us
  other arithmetic  263 us (47%)
  waiting for transfers between devices  166 us (30%)
  matrix products  57.1 us (10%)
  local copies, waits for them, and re-layouts  33.7 us (6%)
  between operations  19.7 us (4%)
    another operation x31, other arithmetic, body(): upper_factor = lax.linalg.cholesky(shifted, symmetrize_input=False).T  173 us
    psum x1, waiting for transfers between devices, body(): packed = lax.psum(pack_upper(masked), ('dof', 'snap'))  154 us
    another operation x9, other arithmetic, body(): lower_factor = jnp.linalg.cholesky(correlation)  37.2 us
    another operation x6, other arithmetic, body(): lax.linalg.triangular_solve(lower_factor, image, left_side=False, lower=T...  31.4 us
    another operation x14, matrix products, body(): upper_factor = lax.linalg.cholesky(shifted, symmetrize_input=False).T  23.2 us
    dot_general x3, matrix products, body(): jnp.dot(shifted, subspace, precision=lax.Precision.HIGHEST, preferred_ele...  16.4 us
    unnamed x16, local copies, waits for them, and re-layouts  14.2 us
    ppermute x3, waiting for transfers between devices, body(): lax.ppermute(sent, 'snap', [(i_2, i_2 ^ step) for i_2 in range(size)])  11.5 us
  transfers between devices with their start and end apart: 4, of which 3 were waited for; matrix products, arithmetic and copies ran while one was open for 2% of the time, Pallas kernels for 0%

profile of v1, /device:TPU:1, one launch (start us, length us, event | category | flops | bytes accessed | tf_op | source)
XLA Modules:
  0.0 543.8 jit_solution(17604062609772087967)
XLA Ops:
  7.3 1.7 constant_dynamic-slice_fusion
  9.0 3.6 collective-permute-start.2
  14.1 4.4 compare_select_fusion.1
  18.6 5.7 %fusion.98 = pred[1024]{0:T(1024)(128)(4,1)S(1)} fusion(pred[1024]{0:T(1024)(128)(4,1)S(1)} %get-tuple-element.30, pred[1024]{0:T(1024)(128)(4,1)S(1)} %get-tuple-element.29, pred[1024]{0:T(1024)(128)(4,1)S(1)} %get-tuple-element.28, pred[1024]{0:T(1024)(128)(4,1)S(1)} %get-tuple-element.27, pred[1024]{0:T(1024)(128)(4,1)S(1)} %get-tuple-element.26, ...), kind=kLoop, calls=%fused_computation.164 | loop fusion | flops 25600 | bytes 18500 | tf_op jit(solution)/shard_map/lt | solution.py:63
  24.3 11.0 %collective-permute-done.2 = bf16[1024,256]{1,0:T(8,128)(2,1)S(1)} collective-permute-done((bf16[1024,256]{1,0:T(8,128)(2,1)S(1)}, bf16[1024,256]{1,0:T(8,128)(2,1)S(1)}, u32[]{:S(2)}, u32[]{:S(2)}) %collective-permute-start.2) | collective-permute-done | bytes 524320 | tf_op jit(solution)/shard_map/ppermute | solution.py:57
  36.1 2.0 gather_fusion
  38.1 4.0 copy.29
  42.1 1.8 bitcast_select_fusion.1
  53.5 154.3 %all-reduce.10.cloned.1.call-done = f32[128,4608]{0,1:T(8,128)} async-done(((f32[128,4608]{0,1:T(8,128)}), f32[128,4608]{0,1:T(8,128)}) %all-reduce.10.cloned.1.call-update) | async-done | bytes 2359312 | tf_op jit(solution)/shard_map/psum | solution.py:66
  208.9 1.9 slice_dynamic-update-slice_fusion
  217.7 5.3 copy.37
  223.0 4.2 fusion.1
  227.2 2.0 copy-done.1
  229.2 11.7 %cholesky.247 = f32[128,128]{1,0:T(8,128)S(1)} custom-call(f32[128,128]{1,0:T(8,128)S(1)} %cholesky.667), custom_call_target="Cholesky" | custom-call | tf_op jit(solution)/shard_map/cholesky | solution.py:69
  241.6 9.8 %custom-call.49 = f32[1,128,128]{1,2,0:T(8,128)S(1)} custom-call(f32[1,128,128]{2,1,0:T(8,128)S(1)} %get-tuple-element.58), custom_call_target="InvertDiagBlocksLowerTriangular" | custom-call | tf_op jit(solution)/shard_map/cholesky | solution.py:69
  251.4 5.4 fusion.107
  258.0 11.7 %cholesky.636 = f32[128,128]{1,0:T(8,128)S(1)} custom-call(f32[128,128]{1,0:T(8,128)S(1)} %fusion.63), custom_call_target="Cholesky" | custom-call | tf_op jit(solution)/shard_map/jit(cholesky)/cholesky | solution.py:83
  271.0 9.8 %custom-call.58 = f32[1,128,128]{1,2,0:T(8,128)S(1)} custom-call(f32[1,128,128]{2,1,0:T(8,128)S(1)} %fusion.46), custom_call_target="InvertDiagBlocksLowerTriangular" | custom-call | tf_op jit(solution)/shard_map/triangular_solve/custom-call.16 | solution.py:84
  281.5 5.4 %fusion.109 = f32[1024,128]{1,0:T(8,128)S(1)} fusion(f32[1024,1024]{1,0:T(8,128)} %copy-done.1, f32[1024,128]{0,1:T(8,128)S(1)} %convolution_bitcast_fusion.2), kind=kOutput, calls=%fused_computation.201 | convolution fusion | flops 1610612736 | bytes 5242880 | tf_op jit(solution)/shard_map/dot_general | solution.py:73
  288.1 11.7 %cholesky.647 = f32[128,128]{1,0:T(8,128)S(1)} custom-call(f32[128,128]{1,0:T(8,128)S(1)} %fusion.61), custom_call_target="Cholesky" | custom-call | tf_op jit(solution)/shard_map/jit(cholesky)/cholesky | solution.py:83
  301.1 9.8 %custom-call.59 = f32[1,128,128]{1,2,0:T(8,128)S(1)} custom-call(f32[1,128,128]{2,1,0:T(8,128)S(1)} %fusion.47), custom_call_target="InvertDiagBlocksLowerTriangular" | custom-call | tf_op jit(solution)/shard_map/triangular_solve/custom-call.16 | solution.py:84
  311.6 5.6 %fusion.111 = f32[1024,128]{1,0:T(8,128)S(1)} fusion(f32[1024,1024]{1,0:T(8,128)} %copy-done.1, f32[1024,128]{0,1:T(8,128)S(1)} %convolution_bitcast_fusion.1), kind=kOutput, calls=%fused_computation.203 | convolution fusion | flops 1610612736 | bytes 5242880 | tf_op jit(solution)/shard_map/dot_general | solution.py:73
  318.3 11.7 %cholesky.658 = f32[128,128]{1,0:T(8,128)S(1)} custom-call(f32[128,128]{1,0:T(8,128)S(1)} %fusion.59), custom_call_target="Cholesky" | custom-call | tf_op jit(solution)/shard_map/jit(cholesky)/cholesky | solution.py:83
  331.4 9.8 %custom-call.60 = f32[1,128,128]{1,2,0:T(8,128)S(1)} custom-call(f32[1,128,128]{2,1,0:T(8,128)S(1)} %fusion.48), custom_call_target="InvertDiagBlocksLowerTriangular" | custom-call | tf_op jit(solution)/shard_map/triangular_solve/custom-call.16 | solution.py:84
  341.9 3.1 fusion.113
  345.0 2.5 cholesky.279
  347.4 2.4 constant_dynamic-update-slice_fusion
  351.4 11.9 %cholesky.270 = f32[128,128]{1,0:T(8,128)S(1)} custom-call(f32[128,128]{1,0:T(8,128)S(1)} %cholesky.671), custom_call_target="Cholesky" | custom-call | tf_op jit(solution)/shard_map/cholesky | solution.py:69
  364.6 9.8 %custom-call.50 = f32[1,128,128]{1,2,0:T(8,128)S(1)} custom-call(f32[1,128,128]{2,1,0:T(8,128)S(1)} %get-tuple-element.55), custom_call_target="InvertDiagBlocksLowerTriangular" | custom-call | tf_op jit(solution)/shard_map/cholesky | solution.py:69
  375.7 2.1 convolution_subtract_fusion.1
  377.8 11.7 %cholesky.493 = f32[128,128]{1,0:T(8,128)S(1)} custom-call(f32[128,128]{1,0:T(8,128)S(1)} %cholesky.676), custom_call_target="Cholesky" | custom-call | tf_op jit(solution)/shard_map/cholesky | solution.py:69
  390.9 10.0 %custom-call.51 = f32[1,128,128]{1,2,0:T(8,128)S(1)} custom-call(f32[1,128,128]{2,1,0:T(8,128)S(1)} %get-tuple-element.52), custom_call_target="InvertDiagBlocksLowerTriangular" | custom-call | tf_op jit(solution)/shard_map/cholesky | solution.py:69
  402.1 2.3 convolution_subtract_fusion.2
  404.4 11.7 %cholesky.512 = f32[128,128]{1,0:T(8,128)S(1)} custom-call(f32[128,128]{1,0:T(8,128)S(1)} %cholesky.681), custom_call_target="Cholesky" | custom-call | tf_op jit(solution)/shard_map/cholesky | solution.py:69
  417.4 9.8 %custom-call.52 = f32[1,128,128]{1,2,0:T(8,128)S(1)} custom-call(f32[1,128,128]{2,1,0:T(8,128)S(1)} %get-tuple-element.49), custom_call_target="InvertDiagBlocksLowerTriangular" | custom-call | tf_op jit(solution)/shard_map/cholesky | solution.py:69
  428.3 2.3 convolution_subtract_fusion.3
  430.6 12.1 %cholesky.531 = f32[128,128]{1,0:T(8,128)S(1)} custom-call(f32[128,128]{1,0:T(8,128)S(1)} %cholesky.686), custom_call_target="Cholesky" | custom-call | tf_op jit(solution)/shard_map/cholesky | solution.py:69
  444.0 9.8 %custom-call.53 = f32[1,128,128]{1,2,0:T(8,128)S(1)} custom-call(f32[1,128,128]{2,1,0:T(8,128)S(1)} %get-tuple-element.46), custom_call_target="InvertDiagBlocksLowerTriangular" | custom-call | tf_op jit(solution)/shard_map/cholesky | solution.py:69
  454.8 2.3 convolution_subtract_fusion.4
  457.1 11.7 %cholesky.551 = f32[128,128]{1,0:T(8,128)S(1)} custom-call(f32[128,128]{1,0:T(8,128)S(1)} %cholesky.691), custom_call_target="Cholesky" | custom-call | tf_op jit(solution)/shard_map/cholesky | solution.py:69
  470.2 9.8 %custom-call.54 = f32[1,128,128]{1,2,0:T(8,128)S(1)} custom-call(f32[1,128,128]{2,1,0:T(8,128)S(1)} %get-tuple-element.43), custom_call_target="InvertDiagBlocksLowerTriangular" | custom-call | tf_op jit(solution)/shard_map/cholesky | solution.py:69
  480.9 2.0 convolution_subtract_fusion.5
  483.0 11.9 %cholesky.571 = f32[128,128]{1,0:T(8,128)S(1)} custom-call(f32[128,128]{1,0:T(8,128)S(1)} %cholesky.696), custom_call_target="Cholesky" | custom-call | tf_op jit(solution)/shard_map/cholesky | solution.py:69
  496.2 9.8 %custom-call.55 = f32[1,128,128]{1,2,0:T(8,128)S(1)} custom-call(f32[1,128,128]{2,1,0:T(8,128)S(1)} %get-tuple-element.40), custom_call_target="InvertDiagBlocksLowerTriangular" | custom-call | tf_op jit(solution)/shard_map/cholesky | solution.py:69
  506.8 1.8 convolution_subtract_fusion.6
  508.6 11.7 %cholesky.589 = f32[128,128]{1,0:T(8,128)S(1)} custom-call(f32[128,128]{1,0:T(8,128)S(1)} %convolution_subtract_fusion.6), custom_call_target="Cholesky" | custom-call | tf_op jit(solution)/shard_map/cholesky | solution.py:69
  526.6 4.8 select_bitcast_fusion
  531.4 5.3 copy.41
  (100 shorter events, 46.9 us)
Async XLA Ops:
  7.2 244.3 %copy-start = (f32[1024,128]{1,0:T(8,128)S(1)}, f32[1024,128]{1,0:T(8,128)}, u32[]{:S(2)}) copy-start(f32[1024,128]{1,0:T(8,128)} %param.10) | copy-start | bytes 1572868
  7.2 6.8 %copy-start.3 = (s32[8,128]{1,0:T(8,128)S(1)}, s32[8,128]{1,0:T(8,128)}, u32[]{:S(2)}) copy-start(s32[8,128]{1,0:T(8,128)} %constant.345.clone.1) | copy-start | bytes 12292
  7.2 6.1 %copy-start.2 = (s32[16]{0:T(128)S(1)}, s32[16]{0:T(128)}, u32[]{:S(2)}) copy-start(s32[16]{0:T(128)} %param.9) | copy-start | bytes 196
  7.2 200.6 %all-reduce.10.cloned.1.call-start = ((), (), s32[]{:S(2)}) async-start(), calls=%async_computation | async-start | bytes 4718592 | tf_op jit(solution)/shard_map/psum | solution.py:66
  9.0 26.4 %collective-permute-start.2 = (bf16[1024,256]{1,0:T(8,128)(2,1)S(1)}, bf16[1024,256]{1,0:T(8,128)(2,1)S(1)}, u32[]{:S(2)}, u32[]{:S(2)}) collective-permute-start(bf16[1024,256]{1,0:T(8,128)(2,1)S(1)} %get-tuple-element.34), channel_id=1, source_target_pairs={{0,3},{1,2},{2,1},{3,0},{4,7},{5,6},{6,5},{7,4},{8,11},{9,10},{10,... | collective-permute-start | bytes 1572872 | tf_op jit(solution)/shard_map/ppermute | solution.py:57
  12.6 22.7 %collective-permute-start.1 = (bf16[1024,256]{1,0:T(8,128)(2,1)S(1)}, bf16[1024,256]{1,0:T(8,128)(2,1)S(1)}, u32[]{:S(2)}, u32[]{:S(2)}) collective-permute-start(bf16[1024,256]{1,0:T(8,128)(2,1)S(1)} %get-tuple-element.35), channel_id=1, source_target_pairs={{0,2},{1,3},{2,0},{3,1},{4,6},{5,7},{6,4},{7,5},{8,10},{9,11},{10,... | collective-permute-start | bytes 1572872 | tf_op jit(solution)/shard_map/ppermute | solution.py:57
  13.0 22.9 %collective-permute-start = (bf16[1024,256]{1,0:T(8,128)(2,1)S(1)}, bf16[1024,256]{1,0:T(8,128)(2,1)S(1)}, u32[]{:S(2)}, u32[]{:S(2)}) collective-permute-start(bf16[1024,256]{1,0:T(8,128)(2,1)S(1)} %get-tuple-element.36), channel_id=1, source_target_pairs={{0,1},{1,0},{2,3},{3,2},{4,5},{5,4},{6,7},{7,6},{8,9},{9,8},{10,11... | collective-permute-start | bytes 1572872 | tf_op jit(solution)/shard_map/ppermute | solution.py:57
  207.8 5.7 %slice-start = ((f32[128,4608]{0,1:T(8,128)}), f32[128,640]{0,1:T(8,128)S(1)}, s32[]{:S(2)}) async-start(f32[128,4608]{0,1:T(8,128)} %all-reduce.10.cloned.1.call-done), calls=%async_computation.1 | async-start | bytes 655360 | tf_op jit(solution)/shard_map/slice | solution.py:42
  207.8 6.6 %slice-start.1 = ((f32[128,4608]{0,1:T(8,128)}), f32[128,512]{0,1:T(8,128)S(1)}, s32[]{:S(2)}) async-start(f32[128,4608]{0,1:T(8,128)} %all-reduce.10.cloned.1.call-done), calls=%async_computation.2 | async-start | bytes 524288 | tf_op jit(solution)/shard_map/slice | solution.py:42
  207.8 7.4 %slice-start.2 = ((f32[128,4608]{0,1:T(8,128)}), f32[128,384]{0,1:T(8,128)S(1)}, s32[]{:S(2)}) async-start(f32[128,4608]{0,1:T(8,128)} %all-reduce.10.cloned.1.call-done), calls=%async_computation.3 | async-start | bytes 393216 | tf_op jit(solution)/shard_map/slice | solution.py:42
  208.9 7.1 %slice-start.3 = ((f32[128,4608]{0,1:T(8,128)}), f32[128,256]{0,1:T(8,128)S(1)}, s32[]{:S(2)}) async-start(f32[128,4608]{0,1:T(8,128)} %all-reduce.10.cloned.1.call-done), calls=%async_computation.4 | async-start | bytes 262144 | tf_op jit(solution)/shard_map/slice | solution.py:42
  208.9 7.9 %slice-start.4 = ((f32[128,4608]{0,1:T(8,128)}), f32[128,128]{0,1:T(8,128)S(1)}, s32[]{:S(2)}) async-start(f32[128,4608]{0,1:T(8,128)} %all-reduce.10.cloned.1.call-done), calls=%async_computation.5 | async-start | bytes 131072 | tf_op jit(solution)/shard_map/slice | solution.py:42
  227.2 2.0 copy-start.1
Sparse Core Ops, SparseCore 0:
  53.6 154.1 all-reduce.9
